TPU v7x, 128 devices: a whole 4x4x4 slice. The times are simulated.
128 devices in a mesh: req: 16 (over y, x), kv: 8 (over z, core).
Axes of the slice: x: 4, y: 4, z: 4, core: 2. Of those that a mesh axis runs over, the one named last changes fastest.
Arguments:
- hidden: bfloat16 [1024, 1536], P('req', 'kv'), may hold values from -6 to 6
- perm: int32 [1024], replicated, may hold values from 0 to 1023, as said below
- seq_lens: int32 [1024], P('req'), may hold values from 1 to 4096, as said below
- page_table: int32 [1024, 32], P('req'), may hold values from 0 to 319, as said below
- kv_cache: bfloat16 [5120, 8, 128, 128], P('req', 'kv'), may hold values from -52 to 52
- attn_gain: float32 [1536], replicated, may hold values from 0.1 to 1.9
- qkv_weight: bfloat16 [8, 1536, 320], P('kv'), may hold values from -0.15625 to 0.15625
- out_weight: bfloat16 [8, 192, 1536], P('kv'), may hold values from -1 to 1
- ffn_gain: float32 [1536], replicated, may hold values from 0.1 to 1.9
- router: bfloat16 [1536, 16], replicated, may hold values from -0.15625 to 0.15625
- routes: int32 [1024, 2], P(('req', 'kv')), may hold values from 0 to 15, all different within a row; in each aligned block of 8 rows (0 to 7, 8 to 15, ...) at most 2 rows name the same one
- gate_up: bfloat16 [16, 1536, 2048], P('req'), may hold values from -0.15625 to 0.15625
- down: bfloat16 [16, 1024, 1536], P('req'), may hold values from -0.1875 to 0.1875
Outputs:
- mixed: bfloat16 [1024, 1536], P(('req', 'kv'))
Inputs may be any that keep to these rules, and one draw needn't show every extreme that they name: A permutation of the 1024 requests: slot s holds request perm[s]. The 64 slots of each index of req hold exactly 4 requests from each block of 64 consecutive requests. `seq_lens`: the length 4096 is reached on every index of req. `page_table`: entries 0 to (seq_lens[s] + 127) // 128 - 1 of row s are used; no page of one index of req is used by two of its slots; later entries name arbitrary pages.
All inputs are finite; a program needn't handle non-finite values.
Results may differ from a plain program's by a relative error of at most 0.017.
Values may be sent and summed in bfloat16 or wider, within the bound.
No kernel may reach another device: no remote copies, remote signals or barrier semaphores. Data moves between devices by JAX's collectives and lax.ppermute only.
A program may use at most 128 MiB of HBM per device.

v0:
```python
import jax
import jax.numpy as jnp
from jax import lax
from jax.sharding import PartitionSpec as P

REQ_DEV = 64
NEG_FILL = -1e30
EPS_NORM = 1e-05


def rms_norm(values, gain_vec):
    values = values.astype(jnp.float32)
    factor = lax.rsqrt(jnp.mean(values * values, axis=-1, keepdims=True) + EPS_NORM)
    return (values * factor * gain_vec).astype(jnp.bfloat16)


def attend(normed, seq_lens, page_table, kv_cache, qkv_weight):
    pool_pages, local_heads, twice_hd, page_len = kv_cache.shape
    head_dim = twice_hd // 2
    slot_count = normed.shape[0]
    groups = qkv_weight.shape[2] // head_dim - 2
    max_pages = page_table.shape[1]
    projected = jnp.einsum("sd,hdc->shc", normed, qkv_weight, preferred_element_type=jnp.float32)
    queries = (
        projected[:, :, : groups * head_dim]
        .reshape(slot_count, local_heads, groups, head_dim)
        .astype(jnp.bfloat16)
    )
    key_new = projected[:, :, groups * head_dim : (groups + 1) * head_dim].astype(jnp.bfloat16)
    value_new = projected[:, :, (groups + 1) * head_dim :].astype(jnp.bfloat16)
    page_need = (seq_lens + page_len - 1) // page_len
    page_ids = jnp.arange(max_pages, dtype=jnp.int32)
    in_use = page_ids[None, :] < page_need[:, None]
    target_page = jnp.where(in_use, page_table, pool_pages).reshape(-1)
    slot_ids = jnp.broadcast_to(
        jnp.arange(slot_count, dtype=jnp.int32)[:, None], (slot_count, max_pages)
    ).reshape(-1)
    order_ids = jnp.broadcast_to(page_ids[None, :], (slot_count, max_pages)).reshape(-1)
    owner = (
        jnp.full((pool_pages,), slot_count, jnp.int32).at[target_page].set(slot_ids, mode="drop")
    )
    page_order = jnp.zeros((pool_pages,), jnp.int32).at[target_page].set(order_ids, mode="drop")
    owner_safe = jnp.minimum(owner, slot_count - 1)
    position = page_order[:, None] * page_len + jnp.arange(page_len, dtype=jnp.int32)[None, :]
    live = (owner[:, None] < slot_count) & (position < jnp.take(seq_lens, owner_safe)[:, None])
    scale_factor = head_dim ** (-0.5)
    page_queries = jnp.take(queries, owner_safe, axis=0)
    scores = (
        jnp.einsum(
            "pkgd,pkdt->pkgt",
            page_queries,
            kv_cache[:, :, :head_dim, :],
            preferred_element_type=jnp.float32,
        )
        * scale_factor
    )
    scores = jnp.where(live[:, None, None, :], scores, NEG_FILL)
    score_new = (
        jnp.einsum("skgd,skd->skg", queries, key_new, preferred_element_type=jnp.float32)
        * scale_factor
    )
    page_peak = jnp.max(scores, axis=3)
    belongs = owner[None, :] == jnp.arange(slot_count, dtype=jnp.int32)[:, None]
    slot_peak = jnp.max(jnp.where(belongs[:, :, None, None], page_peak[None], NEG_FILL), axis=1)
    slot_peak = jnp.maximum(slot_peak, score_new)
    weights = jnp.where(
        live[:, None, None, :],
        jnp.exp(scores - jnp.take(slot_peak, owner_safe, axis=0)[..., None]),
        0.0,
    )
    page_total = jnp.sum(weights, axis=3)
    page_value = jnp.einsum(
        "pkgt,pkdt->pkgd",
        weights.astype(jnp.bfloat16),
        kv_cache[:, :, head_dim:, :],
        preferred_element_type=jnp.float32,
    )
    belongs_f = belongs.astype(jnp.float32)
    total_sum = jnp.dot(
        belongs_f, page_total.reshape(pool_pages, -1), precision=lax.Precision.HIGHEST
    ).reshape(slot_count, local_heads, groups)
    value_sum = jnp.dot(
        belongs_f, page_value.reshape(pool_pages, -1), precision=lax.Precision.HIGHEST
    ).reshape(slot_count, local_heads, groups, head_dim)
    weight_new = jnp.exp(score_new - slot_peak)
    total_sum = total_sum + weight_new
    rounded_new = lax.optimization_barrier(weight_new.astype(jnp.bfloat16)).astype(jnp.float32)
    value_sum = value_sum + rounded_new[..., None] * value_new.astype(jnp.float32)[:, :, None, :]
    return (value_sum / total_sum[..., None]).astype(jnp.bfloat16).reshape(slot_count, -1)


def expert_apply(piece, gate_up, down):
    n_source, slot_num, local_experts, width = piece.shape
    rows_in = piece.transpose(2, 0, 1, 3).reshape(local_experts, n_source * slot_num, width)
    projected_up = jnp.einsum("erd,edf->erf", rows_in, gate_up, preferred_element_type=jnp.float32)
    hidden_units = gate_up.shape[2] // 2
    acts = (
        jax.nn.silu(projected_up[..., :hidden_units]) * projected_up[..., hidden_units:]
    ).astype(jnp.bfloat16)
    result = jnp.einsum("erf,efd->erd", acts, down, preferred_element_type=jnp.float32).astype(
        jnp.bfloat16
    )
    return result.reshape(local_experts, n_source, slot_num, width).transpose(1, 2, 0, 3)


def shards(
    hidden,
    perm,
    seq_lens,
    page_table,
    kv_cache,
    attn_gain,
    qkv_weight,
    out_weight,
    ffn_gain,
    router,
    routes,
    gate_up,
    down,
):
    req_index = lax.axis_index("req")
    kv_index = lax.axis_index("kv")
    every_row = lax.all_gather(hidden, "req", axis=0, tiled=True)
    my_perm = lax.dynamic_slice_in_dim(perm, req_index * REQ_DEV, REQ_DEV)
    picked_rows = jnp.take(every_row, my_perm, axis=0)
    tokens = lax.all_gather(picked_rows, "kv", axis=1, tiled=True)
    normed = rms_norm(tokens, attn_gain)
    head_out = attend(normed, seq_lens, page_table, kv_cache, qkv_weight)
    sub_rows = routes.shape[0]
    width = tokens.shape[1]
    out_flat = out_weight.reshape(-1, out_weight.shape[2])
    attn_rows = lax.psum_scatter(
        jnp.dot(head_out, out_flat, preferred_element_type=jnp.float32).astype(jnp.bfloat16),
        "kv",
        scatter_dimension=0,
        tiled=True,
    ).astype(jnp.float32)
    own_tokens = lax.dynamic_slice_in_dim(tokens, kv_index * sub_rows, sub_rows, 0)
    residual = (own_tokens.astype(jnp.float32) + attn_rows).astype(jnp.bfloat16)
    normed_ffn = rms_norm(residual, ffn_gain)
    logits = jnp.dot(normed_ffn, router, preferred_element_type=jnp.float32)
    chosen = jnp.take_along_axis(logits, routes, axis=1)
    sigmoid_vals = jax.nn.sigmoid(chosen)
    gates = sigmoid_vals / jnp.sum(sigmoid_vals, axis=1, keepdims=True)
    experts_all = router.shape[1]
    n_req = lax.axis_size("req")
    local_experts = gate_up.shape[0]
    capacity = max(2, 2 * sub_rows // experts_all + 1)
    flat_routes = routes.reshape(-1)
    onehot_int = (flat_routes[:, None] == jnp.arange(experts_all, dtype=jnp.int32)[None, :]).astype(
        jnp.int32
    )
    earlier = jnp.cumsum(onehot_int, axis=0) - onehot_int
    rank_in = jnp.sum(earlier * onehot_int, axis=1)
    place_at = (
        flat_routes // local_experts * capacity * local_experts
        + rank_in * local_experts
        + flat_routes % local_experts
    )
    placement_plan = (
        place_at[:, None] == jnp.arange(experts_all * capacity, dtype=jnp.int32)[None, :]
    ).astype(jnp.bfloat16)
    paired_rows = jnp.repeat(normed_ffn, 2, axis=0)
    outgoing = jnp.einsum(
        "qe,qd->ed", placement_plan, paired_rows, preferred_element_type=jnp.float32
    )
    outgoing = outgoing.astype(jnp.bfloat16).reshape(n_req, capacity, local_experts, width)
    arrived = lax.all_to_all(outgoing, "req", split_axis=0, concat_axis=0, tiled=True)
    returned = lax.all_to_all(
        expert_apply(arrived, gate_up, down), "req", split_axis=0, concat_axis=0, tiled=True
    )
    back_rows = returned.reshape(experts_all * capacity, width)
    paired_output = jnp.dot(placement_plan, back_rows, preferred_element_type=jnp.float32).reshape(
        sub_rows, 2, width
    )
    mixed = residual.astype(jnp.float32) + jnp.sum(gates[:, :, None] * paired_output, axis=1)
    return mixed.astype(jnp.bfloat16)


def solution(mesh):
    in_specs = (
        P("req", "kv"),
        P(),
        P("req"),
        P("req", None),
        P("req", "kv", None, None),
        P(),
        P("kv", None, None),
        P("kv", None, None),
        P(),
        P(),
        P(("req", "kv"), None),
        P("req", None, None),
        P("req", None, None),
    )
    out_specs = P(("req", "kv"), None)
    return jax.shard_map(shards, mesh=mesh, in_specs=in_specs, out_specs=out_specs, check_vma=False)
```

profile of v0, /device:TPU:0, one launch (start us, length us, event | category | flops | bytes accessed | tf_op | source)
XLA Modules:
  0.0 223.6 jit_solution(11353303705725707446)
XLA Ops:
  6.5 2.1 fusion.66
  8.6 2.1 fusion.67
  10.7 2.1 fusion.68
  12.8 0.7 and_select_fusion
  13.4 1.6 fusion.69
  15.0 0.7 fusion.51
  16.0 8.0 %scatter_custom_fusion = s32[320]{0:T(512)S(1)} fusion(s32[2048]{0:T(1024)S(1)} %bitcast.180, s32[2048]{0:T(1024)S(1)} %reshape.468, s32[]{:T(128)} %constant.102.clone.1), kind=kCustom, calls=%fused_computation.112 | custom fusion | bytes 1284 | tf_op jit(solution)/shard_map/scatter | solution.py:40
  24.1 0.6 broadcast_compare_fusion
  24.7 0.6 compare_select_fusion.2
  25.2 0.8 compare_and_fusion.1
  26.0 26.8 %all_gather.6 = bf16[1024,192]{1,0:T(8,128)(2,1)} all-gather(bf16[64,192]{1,0:T(8,128)(2,1)} %param.13), channel_id=1, replica_groups=mesh['req'=16,'kv'=8] {'req'}, dimensions={0}, use_global_device_ids=true | all-gather | bytes 417792 | tf_op jit(solution)/shard_map/all_gather | solution.py:123
  52.8 1.8 gather_fusion
  54.7 14.0 %all-gather = bf16[8,192,64]{1,2,0:T(8,128)(2,1)S(1)} all-gather(bf16[1,192,64]{1,2,0:T(8,128)(2,1)S(1)} %select_bitcast_fusion), channel_id=1, replica_groups=mesh['req'=16,'kv'=8] {'kv'}, dimensions={0}, use_global_device_ids=true | all-gather | bytes 221184 | tf_op jit(solution)/shard_map/all_gather | solution.py:126
  68.7 0.9 copy.104
  69.6 1.2 reshape.494
  70.9 1.7 convolution_bitcast_fusion
  72.6 0.7 fusion.50
  73.3 8.2 %scatter_custom_fusion.1 = s32[320]{0:T(512)S(1)} fusion(s32[2048]{0:T(1024)S(1)} %bitcast.181, s32[2048]{0:T(1024)S(1)} %reshape.476, s32[]{:T(128)} %constant.106.clone.1), kind=kCustom, calls=%fused_computation.109 | custom fusion | bytes 1284 | tf_op jit(solution)/shard_map/scatter | solution.py:42
  81.6 0.6 broadcast_multiply_fusion
  82.4 0.7 pad_clamp_fusion
  83.1 2.5 %gather_fusion.1 = bf16[320,3,64]{2,1,0:T(4,128)(2,1)} fusion(bf16[64,3,64]{2,1,0:T(4,128)(2,1)S(1)} %copy.107, s32[1024]{0:T(1024)S(1)} %pad_clamp_fusion), kind=kCustom, calls=%fused_computation.1 | custom fusion | bytes 247040 | tf_op jit(solution)/shard_map/jit(_take)/gather | solution.py:47
  85.5 39.8 %select_select_fusion = s32[320]{0:T(512)S(1)} fusion(s32[]{:T(128)} %bitcast.5, s32[]{:T(128)} %bitcast.6, s32[]{:T(128)} %bitcast.7, s32[]{:T(128)} %bitcast.8, s32[]{:T(128)} %bitcast.9, s32[]{:T(128)} %bitcast.10, s32[]{:T(128)} %bitcast.11, s32[]{:T(128)} %bitcast.12, s32[]{:T(128)} %bitcast.13, s32[]{:T(128)} %bitcast.14, s32[]{:T(128)} %bitcast.15, ...), kind=kLoop, calls=%fused_computation.96 | loop fusion | flops 42880 | bytes 2816 | tf_op jit(solution)/shard_map/jit(_take)/select_n | solution.py:45
  125.4 0.9 fusion.36
  126.3 5.7 %fusion.70 = (f32[320,3]{1,0:T(8,128)}, f32[320,3,128]{2,1,0:T(4,128)}) fusion(bf16[320,1,128,128]{3,2,0,1:T(8,128)(2,1)} %bitcast.182, bf16[320,3,64]{2,1,0:T(4,128)(2,1)} %gather_fusion.1, pred[320]{0:T(512)(128)(4,1)} %get-tuple-element.16, pred[320,128]{1,0:T(8,128)(4,1)S(1)} %fusion.36), kind=kOutput, calls=%fused_computation.124 | convolution fusion | flops 16157760 | bytes 6107392 | tf_op jit(solution)/shard_map/pkgd,pkdt->pkgt/dot_general | solution.py:49
  131.9 1.0 copy.109
  132.9 0.9 fusion.48
  134.2 1.6 gather_fusion.2
  135.8 1.0 broadcast_select_fusion
  136.9 1.9 fusion.19
  138.8 6.5 %fusion.2 = f32[320,3,64]{2,1,0:T(4,128)} fusion(bf16[320,1,128,128]{3,2,0,1:T(8,128)(2,1)} %bitcast.183, f32[320,3,128]{2,1,0:T(4,128)} %get-tuple-element.82, f32[320,3]{1,0:T(8,128)S(1)} %broadcast_select_fusion, pred[320,128]{1,0:T(8,128)(4,1)S(1)} %fusion.36), kind=kOutput, calls=%fused_computation.9 | convolution fusion | flops 16097280 | bytes 6188800 | tf_op jit(solution)/shard_map/pkgt,pkdt->pkgd/dot_general | solution.py:72
  145.2 0.2 convolution_add_fusion.1
  145.5 2.1 copy.112
  147.5 2.0 fusion.15
  149.5 0.9 copy.113
  150.4 2.0 convolution_convert_fusion
  153.3 28.5 %reduce-scatter.2.cloned.1.call-done = bf16[8,1536]{1,0:T(8,128)(2,1)} async-done(((bf16[64,1536]{1,0:T(8,128)(2,1)}), bf16[8,1536]{1,0:T(8,128)(2,1)}) %reduce-scatter.2.cloned.1.call-update) | async-done | bytes 24592 | tf_op jit(solution)/shard_map/reduce_scatter | solution.py:132
  181.9 0.9 fusion.41
  182.9 0.7 gather_fusion.3
  183.7 0.3 convolution_convert_fusion.1
  184.0 0.7 reshape.351
  184.7 6.8 %all-to-all-start = ((bf16[16,2,1,1536]{3,1,2,0:T(2,128)(2,1)}), bf16[16,2,1,1536]{3,1,2,0:T(2,128)(2,1)S(1)}, u32[]{:S(2)}, u32[]{:S(2)}) async-start(bf16[16,2,1,1536]{3,1,2,0:T(2,128)(2,1)} %bitcast.90), calls=%async_computation.1 | async-start | bytes 196608 | tf_op jit(solution)/shard_map/all_to_all | solution.py:168
  191.7 7.7 %all-to-all-done = bf16[16,2,1,1536]{3,1,2,0:T(2,128)(2,1)S(1)} async-done(((bf16[16,2,1,1536]{3,1,2,0:T(2,128)(2,1)}), bf16[16,2,1,1536]{3,1,2,0:T(2,128)(2,1)S(1)}, u32[]{:S(2)}, u32[]{:S(2)}) %all-to-all-start) | async-done | bytes 98336 | tf_op jit(solution)/shard_map/all_to_all | solution.py:168
  199.4 4.0 %fusion.6 = f32[1,32,2048]{2,1,0:T(8,128)S(1)} fusion(bf16[32,1536]{1,0:T(8,128)(2,1)S(1)} %reshape.352, bf16[1,1536,2048]{2,1,0:T(8,128)(2,1)} %param.24), kind=kOutput, calls=%fused_computation.15 | convolution fusion | flops 201326592 | bytes 6651904 | tf_op jit(solution)/shard_map/erd,edf->erf/dot_general | solution.py:95
  203.4 0.6 fusion.9
  204.0 0.7 transpose_reshape.3
  204.6 3.5 %all-to-all-start.1 = ((bf16[16,2,1,1536]{3,1,2,0:T(2,128)(2,1)}), bf16[16,2,1,1536]{3,1,2,0:T(2,128)(2,1)S(1)}, u32[]{:S(2)}, u32[]{:S(2)}) async-start(bf16[16,2,1,1536]{3,1,2,0:T(2,128)(2,1)} %bitcast.95), calls=%async_computation.2 | async-start | bytes 196608 | tf_op jit(solution)/shard_map/all_to_all | solution.py:169
  208.3 7.6 %all-to-all-done.1 = bf16[16,2,1,1536]{3,1,2,0:T(2,128)(2,1)S(1)} async-done(((bf16[16,2,1,1536]{3,1,2,0:T(2,128)(2,1)}), bf16[16,2,1,1536]{3,1,2,0:T(2,128)(2,1)S(1)}, u32[]{:S(2)}, u32[]{:S(2)}) %all-to-all-start.1) | async-done | bytes 98336 | tf_op jit(solution)/shard_map/all_to_all | solution.py:169
  216.2 0.6 fusion.44
  (55 shorter events, 3.0 us)
Async XLA Ops:
  6.5 196.8 %copy-start = (bf16[1,1024,1536]{2,1,0:T(8,128)(2,1)S(1)}, bf16[1,1024,1536]{2,1,0:T(8,128)(2,1)}, u32[]{:S(2)}) copy-start(bf16[1,1024,1536]{2,1,0:T(8,128)(2,1)} %param.25) | copy-start | bytes 9437188
  6.5 175.3 %reduce-scatter.2.cloned.1.call-start = ((), (), s32[]{:S(2)}) async-start(), calls=%async_computation.3 | async-start | bytes 221184 | tf_op jit(solution)/shard_map/reduce_scatter | solution.py:132
  134.2 18.2 %copy-start.3 = (s32[8,2]{0,1:T(2,128)S(1)}, s32[8,2]{0,1:T(2,128)}, u32[]{:S(2)}) copy-start(s32[8,2]{0,1:T(2,128)} %param.23) | copy-start | bytes 196
  134.2 48.5 %copy-start.2 = (f32[1536]{0:T(1024)S(1)}, f32[1536]{0:T(1024)}, u32[]{:S(2)}) copy-start(f32[1536]{0:T(1024)} %param.21) | copy-start | bytes 18436
  134.2 48.6 %copy-start.1 = (bf16[1536,16]{0,1:T(8,128)(2,1)S(1)}, bf16[1536,16]{0,1:T(8,128)(2,1)}, u32[]{:S(2)}) copy-start(bf16[1536,16]{0,1:T(8,128)(2,1)} %param.22) | copy-start | bytes 147460
  184.7 14.6 %all-to-all-start = ((bf16[16,2,1,1536]{3,1,2,0:T(2,128)(2,1)}), bf16[16,2,1,1536]{3,1,2,0:T(2,128)(2,1)S(1)}, u32[]{:S(2)}, u32[]{:S(2)}) async-start(bf16[16,2,1,1536]{3,1,2,0:T(2,128)(2,1)} %bitcast.90), calls=%async_computation.1 | async-start | bytes 196608 | tf_op jit(solution)/shard_map/all_to_all | solution.py:168
  204.6 11.3 %all-to-all-start.1 = ((bf16[16,2,1,1536]{3,1,2,0:T(2,128)(2,1)}), bf16[16,2,1,1536]{3,1,2,0:T(2,128)(2,1)S(1)}, u32[]{:S(2)}, u32[]{:S(2)}) async-start(bf16[16,2,1,1536]{3,1,2,0:T(2,128)(2,1)} %bitcast.95), calls=%async_computation.2 | async-start | bytes 196608 | tf_op jit(solution)/shard_map/all_to_all | solution.py:169
Sparse Core Ops, SparseCore 0:
  152.5 29.2 reduce-scatter.1
where the time goes:
time: 225 us; the launch traced here: 224 us
  other arithmetic  51.4 us (23%)
  waiting for transfers between devices  43.9 us (20%)
  blocking collectives  40.8 us (18%)
  local copies, waits for them, and re-layouts  39.5 us (18%)
  matrix products  24.1 us (11%)
  between operations  13.6 us (6%)
  starting transfers between devices  10.3 us (5%)
    select_n x2, other arithmetic, attend(): jnp.take(seq_lens, owner_safe)[:, None]  40.4 us
    reduce_scatter x1, waiting for transfers between devices, shards(): lax.psum_scatter(jnp.dot(head_out, out_flat, preferred_element_type=jnp.f...  28.5 us
    all_gather x1, blocking collectives, shards(): every_row = lax.all_gather(hidden, 'req', axis=0, tiled=True)  26.8 us
    all_gather x1, blocking collectives, shards(): tokens = lax.all_gather(picked_rows, 'kv', axis=1, tiled=True)  14 us
    scatter x1, local copies, waits for them, and re-layouts, attend(): jnp.zeros((pool_pages,), jnp.int32).at[target_page]  8.21 us
    scatter x1, local copies, waits for them, and re-layouts, attend(): jnp.full((pool_pages,), slot_count, jnp.int32).at[target_page]  8.03 us
    gather x4, local copies, waits for them, and re-layouts, attend(): jnp.take(seq_lens, owner_safe)[:, None]  7.79 us
    all_to_all x1, waiting for transfers between devices, shards(): lax.all_to_all(outgoing, 'req', split_axis=0, concat_axis=0, tiled=True)  7.69 us
  transfers between devices with their start and end apart: 3, of which 3 were waited for; matrix products, arithmetic and copies ran while one was open for 1% of the time, Pallas kernels for 0%

commit v1 on v0

--- a/solution.py
+++ b/solution.py
@@ -120,7 +120,9 @@
 ):
     req_index = lax.axis_index("req")
     kv_index = lax.axis_index("kv")
-    every_row = lax.all_gather(hidden, "req", axis=0, tiled=True)
+    every_row = jnp.concatenate(
+        lax.all_to_all(jnp.stack([hidden] * lax.axis_size("req")), "req", 0, 0), axis=0
+    )
     my_perm = lax.dynamic_slice_in_dim(perm, req_index * REQ_DEV, REQ_DEV)
     picked_rows = jnp.take(every_row, my_perm, axis=0)
     tokens = lax.all_gather(picked_rows, "kv", axis=1, tiled=True)

time: 225 us -> 208 us (0.924)
  blocking collectives: 40.8 us -> 14.2 us
  starting transfers between devices: 10.3 us -> 17.5 us
  local copies, waits for them, and re-layouts: 39.5 us -> 41.9 us
    all_gather x1 -> x0, blocking collectives: 26.8 us -> none  [shards(): every_row = lax.all_gather(hidden, 'req', axis=0, tiled=True)]
    all_to_all x0 -> x1, starting transfers between devices: none -> 7.17 us  [shards(): lax.all_to_all(jnp.stack([hidden] * lax.axis_size('req')), 'req', 0, 0)]
  transfers between devices with their start and end apart: 3 -> 4, of which waited for: 3 -> 3; matrix products, arithmetic and copies ran while one was open for 1% -> 35% of each run, Pallas kernels for 0% -> 0%
where the time goes in v1:
time: 208 us; the launch traced here: 207 us
  other arithmetic  50.5 us (24%)
  waiting for transfers between devices  45.2 us (22%)
  local copies, waits for them, and re-layouts  41.9 us (20%)
  matrix products  23.5 us (11%)
  starting transfers between devices  17.5 us (8%)
  blocking collectives  14.2 us (7%)
  between operations  13.8 us (7%)
    select_n x2, other arithmetic, attend(): jnp.take(seq_lens, owner_safe)[:, None]  39.8 us
    reduce_scatter x1, waiting for transfers between devices, shards(): lax.psum_scatter(jnp.dot(head_out, out_flat, preferred_element_type=jnp.f...  29.8 us
    all_gather x1, blocking collectives, shards(): tokens = lax.all_gather(picked_rows, 'kv', axis=1, tiled=True)  14.2 us
    scatter x1, local copies, waits for them, and re-layouts, attend(): jnp.full((pool_pages,), slot_count, jnp.int32).at[target_page]  8.03 us
    scatter x1, local copies, waits for them, and re-layouts, attend(): jnp.zeros((pool_pages,), jnp.int32).at[target_page]  8.03 us
    gather x4, local copies, waits for them, and re-layouts, attend(): jnp.take(seq_lens, owner_safe)[:, None]  7.8 us
    all_to_all x1, waiting for transfers between devices, shards(): lax.all_to_all(outgoing, 'req', split_axis=0, concat_axis=0, tiled=True)  7.69 us
    all_to_all x1, waiting for transfers between devices, shards(): lax.all_to_all(expert_apply(arrived, gate_up, down), 'req', split_axis=0,...  7.62 us
  transfers between devices with their start and end apart: 4, of which 3 were waited for; matrix products, arithmetic and copies ran while one was open for 35% of the time, Pallas kernels for 0%

profile of v1, /device:TPU:0, one launch (start us, length us, event | category | flops | bytes accessed | tf_op | source)
XLA Modules:
  0.0 206.5 jit_solution(13463860583436728761)
XLA Ops:
  6.5 1.8 stack.2
  8.3 7.2 %all-to-all-start = ((bf16[16,64,192]{2,1,0:T(8,128)(2,1)}), bf16[16,64,192]{2,1,0:T(8,128)(2,1)}, u32[]{:S(2)}, u32[]{:S(2)}) async-start(bf16[16,64,192]{2,1,0:T(8,128)(2,1)} %stack.2), calls=%async_computation | async-start | bytes 1048576 | tf_op jit(solution)/shard_map/all_to_all | solution.py:124
  15.5 2.1 fusion.66
  17.6 2.1 %fusion.67 = (s32[1]{0:T(128)}, s32[1]{0:T(128)}, s32[1]{0:T(128)}, s32[1]{0:T(128)}, s32[1]{0:T(128)}, /*index=5*/s32[1]{0:T(128)}, s32[1]{0:T(128)}, s32[1]{0:...) fusion(s32[64]{0:T(128)} %param.15), kind=kLoop, calls=%fused_computation.121 | loop fusion | bytes 152 | tf_op jit(solution)/shard_map/jit(_take)/gather | solution.py:45
  19.7 2.1 %fusion.68 = (s32[1]{0:T(128)}, s32[1]{0:T(128)}, s32[1]{0:T(128)}, s32[1]{0:T(128)}, s32[1]{0:T(128)}, /*index=5*/s32[1]{0:T(128)}, s32[1]{0:T(128)}, s32[1]{0:...) fusion(s32[64]{0:T(128)} %param.15), kind=kLoop, calls=%fused_computation.122 | loop fusion | bytes 152 | tf_op jit(solution)/shard_map/jit(_take)/gather | solution.py:45
  21.8 0.7 and_select_fusion
  22.4 1.6 fusion.69
  24.0 0.7 fusion.51
  25.0 8.0 %scatter_custom_fusion = s32[320]{0:T(512)S(1)} fusion(s32[2048]{0:T(1024)S(1)} %bitcast.181, s32[2048]{0:T(1024)S(1)} %reshape.474, s32[]{:T(128)} %constant.102.clone.1), kind=kCustom, calls=%fused_computation.112 | custom fusion | bytes 1284 | tf_op jit(solution)/shard_map/scatter | solution.py:40
  33.2 8.0 %scatter_custom_fusion.1 = s32[320]{0:T(512)S(1)} fusion(s32[2048]{0:T(1024)S(1)} %bitcast.182, s32[2048]{0:T(1024)S(1)} %reshape.482, s32[]{:T(128)} %constant.106.clone.1), kind=kCustom, calls=%fused_computation.109 | custom fusion | bytes 1284 | tf_op jit(solution)/shard_map/scatter | solution.py:42
  41.3 0.8 copy.114
  42.5 0.6 multiply_add_fusion
  43.1 0.8 compare_and_fusion.1
  43.9 39.8 %select_select_fusion = s32[320]{0:T(512)S(1)} fusion(s32[]{:T(128)} %bitcast.6, s32[]{:T(128)} %bitcast.7, s32[]{:T(128)} %bitcast.8, s32[]{:T(128)} %bitcast.9, s32[]{:T(128)} %bitcast.10, s32[]{:T(128)} %bitcast.11, s32[]{:T(128)} %bitcast.12, s32[]{:T(128)} %bitcast.13, s32[]{:T(128)} %bitcast.14, s32[]{:T(128)} %bitcast.15, s32[]{:T(128)} %bitcast.16, ...), kind=kLoop, calls=%fused_computation.96 | loop fusion | flops 42880 | bytes 2816 | tf_op jit(solution)/shard_map/jit(_take)/select_n | solution.py:45
  83.7 0.7 copy.117
  84.6 1.8 gather_fusion
  86.5 14.2 %all-gather = bf16[8,192,64]{1,2,0:T(8,128)(2,1)S(1)} all-gather(bf16[1,192,64]{1,2,0:T(8,128)(2,1)S(1)} %select_bitcast_fusion), channel_id=1, replica_groups=mesh['req'=16,'kv'=8] {'kv'}, dimensions={0}, use_global_device_ids=true | all-gather | bytes 221184 | tf_op jit(solution)/shard_map/all_gather | solution.py:128
  100.7 0.8 copy.104
  101.5 1.2 reshape.500
  102.9 1.7 convolution_bitcast_fusion
  104.5 0.7 fusion.50
  105.5 2.5 %gather_fusion.1 = bf16[320,3,64]{2,1,0:T(4,128)(2,1)} fusion(bf16[64,3,64]{2,1,0:T(4,128)(2,1)S(1)} %copy.107, s32[1024]{0:T(1024)S(1)} %pad_clamp_fusion), kind=kCustom, calls=%fused_computation.1 | custom fusion | bytes 247040 | tf_op jit(solution)/shard_map/jit(_take)/gather | solution.py:47
  107.9 5.7 %fusion.70 = (f32[320,3]{1,0:T(8,128)}, f32[320,3,128]{2,1,0:T(4,128)}) fusion(bf16[320,1,128,128]{3,2,0,1:T(8,128)(2,1)} %bitcast.183, bf16[320,3,64]{2,1,0:T(4,128)(2,1)} %gather_fusion.1, pred[320]{0:T(512)(128)(4,1)S(1)} %get-tuple-element.16, pred[320,128]{1,0:T(8,128)(4,1)S(1)} %fusion.36), kind=kOutput, calls=%fused_computation.124 | convolution fusion | flops 16157760 | bytes 6107200 | tf_op jit(solution)/shard_map/pkgd,pkdt->pkgt/dot_general | solution.py:49
  113.6 1.0 copy.109
  114.6 0.9 fusion.48
  115.8 0.6 convert_bitcast_fusion
  116.4 1.2 gather_fusion.2
  117.7 0.7 broadcast_select_fusion
  118.4 1.9 fusion.19
  120.3 6.5 %fusion.2 = f32[320,3,64]{2,1,0:T(4,128)} fusion(bf16[320,1,128,128]{3,2,0,1:T(8,128)(2,1)} %bitcast.184, f32[320,3,128]{2,1,0:T(4,128)} %get-tuple-element.82, f32[320,3]{1,0:T(8,128)S(1)} %broadcast_select_fusion, pred[320,128]{1,0:T(8,128)(4,1)} %copy-done.1), kind=kOutput, calls=%fused_computation.9 | convolution fusion | flops 16097280 | bytes 6188800 | tf_op jit(solution)/shard_map/pkgt,pkdt->pkgd/dot_general | solution.py:72
  127.1 2.1 %copy.112 = f32[320,3,64]{0,2,1:T(8,128)} copy(f32[320,3,64]{2,1,0:T(4,128)} %fusion.2) | data formatting | bytes 491520 | tf_op jit(solution)/shard_map/pkgt,pkdt->pkgd/dot_general | solution.py:72
  129.2 1.3 fusion.15
  130.6 2.0 convolution_convert_fusion
  132.6 0.7 bitcast_or_fusion
  133.5 0.8 copy.122
  134.3 0.7 multiply_add_fusion.1
  134.9 29.8 %reduce-scatter.2.cloned.1.call-done = bf16[8,1536]{1,0:T(8,128)(2,1)} async-done(((bf16[64,1536]{1,0:T(8,128)(2,1)}), bf16[8,1536]{1,0:T(8,128)(2,1)}) %reduce-scatter.2.cloned.1.call-update) | async-done | bytes 24592 | tf_op jit(solution)/shard_map/reduce_scatter | solution.py:134
  164.8 0.9 fusion.41
  165.8 0.7 gather_fusion.3
  166.9 0.7 reshape.357
  167.6 6.8 %all-to-all-start.1 = ((bf16[16,2,1,1536]{3,1,2,0:T(2,128)(2,1)}), bf16[16,2,1,1536]{3,1,2,0:T(2,128)(2,1)S(1)}, u32[]{:S(2)}, u32[]{:S(2)}) async-start(bf16[16,2,1,1536]{3,1,2,0:T(2,128)(2,1)} %bitcast.91), calls=%async_computation.2 | async-start | bytes 196608 | tf_op jit(solution)/shard_map/all_to_all | solution.py:170
  174.5 7.7 %all-to-all-done.1 = bf16[16,2,1,1536]{3,1,2,0:T(2,128)(2,1)S(1)} async-done(((bf16[16,2,1,1536]{3,1,2,0:T(2,128)(2,1)}), bf16[16,2,1,1536]{3,1,2,0:T(2,128)(2,1)S(1)}, u32[]{:S(2)}, u32[]{:S(2)}) %all-to-all-start.1) | async-done | bytes 98336 | tf_op jit(solution)/shard_map/all_to_all | solution.py:170
  182.3 4.0 %fusion.6 = f32[1,32,2048]{2,1,0:T(8,128)S(1)} fusion(bf16[32,1536]{1,0:T(8,128)(2,1)S(1)} %reshape.358, bf16[1,1536,2048]{2,1,0:T(8,128)(2,1)} %param.24), kind=kOutput, calls=%fused_computation.15 | convolution fusion | flops 201326592 | bytes 6651904 | tf_op jit(solution)/shard_map/erd,edf->erf/dot_general | solution.py:95
  186.2 0.6 fusion.9
  186.9 0.7 transpose_reshape.3
  187.5 3.5 %all-to-all-start.2 = ((bf16[16,2,1,1536]{3,1,2,0:T(2,128)(2,1)}), bf16[16,2,1,1536]{3,1,2,0:T(2,128)(2,1)S(1)}, u32[]{:S(2)}, u32[]{:S(2)}) async-start(bf16[16,2,1,1536]{3,1,2,0:T(2,128)(2,1)} %bitcast.96), calls=%async_computation.3 | async-start | bytes 196608 | tf_op jit(solution)/shard_map/all_to_all | solution.py:171
  191.2 7.6 %all-to-all-done.2 = bf16[16,2,1,1536]{3,1,2,0:T(2,128)(2,1)S(1)} async-done(((bf16[16,2,1,1536]{3,1,2,0:T(2,128)(2,1)}), bf16[16,2,1,1536]{3,1,2,0:T(2,128)(2,1)S(1)}, u32[]{:S(2)}, u32[]{:S(2)}) %all-to-all-start.2) | async-done | bytes 98336 | tf_op jit(solution)/shard_map/all_to_all | solution.py:171
  199.1 0.6 fusion.44
  (69 shorter events, 3.6 us)
Async XLA Ops:
  6.5 179.7 %copy-start = (bf16[1,1024,1536]{2,1,0:T(8,128)(2,1)S(1)}, bf16[1,1024,1536]{2,1,0:T(8,128)(2,1)}, u32[]{:S(2)}) copy-start(bf16[1,1024,1536]{2,1,0:T(8,128)(2,1)} %param.25) | copy-start | bytes 9437188
  8.3 76.3 %all-to-all-start = ((bf16[16,64,192]{2,1,0:T(8,128)(2,1)}), bf16[16,64,192]{2,1,0:T(8,128)(2,1)}, u32[]{:S(2)}, u32[]{:S(2)}) async-start(bf16[16,64,192]{2,1,0:T(8,128)(2,1)} %stack.2), calls=%async_computation | async-start | bytes 1048576 | tf_op jit(solution)/shard_map/all_to_all | solution.py:124
  15.5 149.3 %reduce-scatter.2.cloned.1.call-start = ((), (), s32[]{:S(2)}) async-start(), calls=%async_computation.4 | async-start | bytes 221184 | tf_op jit(solution)/shard_map/reduce_scatter | solution.py:134
  33.1 81.5 %copy-start.8 = (pred[320]{0:T(512)(128)(4,1)}, pred[320]{0:T(512)(128)(4,1)S(1)}, u32[]{:S(2)}) copy-start(pred[320]{0:T(512)(128)(4,1)S(1)} %get-tuple-element.16) | copy-start | bytes 964
  42.1 42.5 %copy-start.6 = (s32[16]{0:T(128)}, s32[16]{0:T(128)S(1)}, u32[]{:S(2)}) copy-start(s32[16]{0:T(128)S(1)} %eq.72) | copy-start | bytes 196
  42.4 41.3 %copy-start.9 = (s32[16]{0:T(128)}, s32[16]{0:T(128)S(1)}, u32[]{:S(2)}) copy-start(s32[16]{0:T(128)S(1)} %select_reduce_fusion.1) | copy-start | bytes 196
  84.4 32.0 %copy-start.4 = (s32[1024]{0:T(1024)}, s32[1024]{0:T(1024)S(1)}, u32[]{:S(2)}) copy-start(s32[1024]{0:T(1024)S(1)} %pad_clamp_fusion) | copy-start | bytes 12292
  84.6 31.8 %copy-start.1 = (pred[320,128]{1,0:T(8,128)(4,1)}, pred[320,128]{1,0:T(8,128)(4,1)S(1)}, u32[]{:S(2)}) copy-start(pred[320,128]{1,0:T(8,128)(4,1)S(1)} %fusion.36) | copy-start | bytes 122884
  117.7 11.5 %copy-start.3 = (f32[64,64]{1,0:T(8,128)S(1)}, f32[64,64]{1,0:T(8,128)}, u32[]{:S(2)}) copy-start(f32[64,64]{1,0:T(8,128)} %get-tuple-element.9) | copy-start | bytes 49156
  118.4 10.7 %copy-start.7 = (bf16[64,1,3]{0,2,1:T(4,128)(2,1)S(1)}, bf16[64,1,3]{0,2,1:T(4,128)(2,1)}, u32[]{:S(2)}) copy-start(bf16[64,1,3]{0,2,1:T(4,128)(2,1)} %get-tuple-element.13) | copy-start | bytes 1156
  118.4 47.2 %copy-start.5 = (f32[1536]{0:T(1024)S(1)}, f32[1536]{0:T(1024)}, u32[]{:S(2)}) copy-start(f32[1536]{0:T(1024)} %param.21) | copy-start | bytes 18436
  118.4 47.3 %copy-start.2 = (bf16[1536,16]{0,1:T(8,128)(2,1)S(1)}, bf16[1536,16]{0,1:T(8,128)(2,1)}, u32[]{:S(2)}) copy-start(bf16[1536,16]{0,1:T(8,128)(2,1)} %param.22) | copy-start | bytes 147460
  167.6 14.6 %all-to-all-start.1 = ((bf16[16,2,1,1536]{3,1,2,0:T(2,128)(2,1)}), bf16[16,2,1,1536]{3,1,2,0:T(2,128)(2,1)S(1)}, u32[]{:S(2)}, u32[]{:S(2)}) async-start(bf16[16,2,1,1536]{3,1,2,0:T(2,128)(2,1)} %bitcast.91), calls=%async_computation.2 | async-start | bytes 196608 | tf_op jit(solution)/shard_map/all_to_all | solution.py:170
  187.5 11.3 %all-to-all-start.2 = ((bf16[16,2,1,1536]{3,1,2,0:T(2,128)(2,1)}), bf16[16,2,1,1536]{3,1,2,0:T(2,128)(2,1)S(1)}, u32[]{:S(2)}, u32[]{:S(2)}) async-start(bf16[16,2,1,1536]{3,1,2,0:T(2,128)(2,1)} %bitcast.96), calls=%async_computation.3 | async-start | bytes 196608 | tf_op jit(solution)/shard_map/all_to_all | solution.py:171
Sparse Core Ops, SparseCore 0:
  132.8 31.9 reduce-scatter.1
